TPU v7x, 512 devices: a whole 4x4x16 slice. The times are simulated.
512 devices in a mesh: acq: 16 (over y_lo, x, core), pulse: 32 (over y_hi, z).
Axes of the slice: x: 4, y: 4 (y_hi: 2, y_lo: 2; y = y_hi * 2 + y_lo), z: 16, core: 2. Of those that a mesh axis runs over, the one named last changes fastest.
Arguments:
- raw_echo: bfloat16 [16, 2, 8192, 1535], P('acq', None, 'pulse'), may hold values from -6 to 6
- chirp_phase: float32 [1024], replicated, may hold values from -3.140625 to 3.140625
- pulse_counts: int32 [16], P('acq'), may hold values from 4096 to 8192, as said below
- azimuth_rate: float32 [512], P('pulse'), may hold values from 0.25 to 1
- partner_bits: int32 [16, 2], P('acq'), may hold values from 0 to 3, as said below
Outputs:
- interfere_real: float32 [16, 2, 128, 512], P('acq', None, 'pulse')
- interfere_imag: float32 [16, 2, 128, 512], P('acq', None, 'pulse')
Inputs may be any that keep to these rules, and one draw needn't show every extreme that they name: `pulse_counts`: at least half of 8192; some acquisition records all 8192 pulses and some exactly half. `partner_bits`: the two bits of a row differ.
All inputs are finite; a program needn't handle non-finite values.
Results may differ from a plain program's by a relative error of at most 0.0065.
Values may be sent and summed in bfloat16 or wider, within the bound.
No kernel may reach another device: no remote copies, remote signals or barrier semaphores. Data moves between devices by JAX's collectives and lax.ppermute only.
A program may use at most 64 MiB of HBM per device.

v0:
```python
import math
import jax
import jax.numpy as jnp
from jax import lax
from jax.sharding import PartitionSpec as P

RNG = 512
TAPS = 1024
LOOK_RNG = 4
LOOK_AZ = 16


def part_tables(length, inverse):
    steps = jnp.arange(length, dtype=jnp.int32)
    angle = 2.0 * jnp.pi * (steps[:, None] * steps[None, :] % length).astype(jnp.float32) / length
    cosine = jnp.cos(angle)
    sine = jnp.sin(angle)
    if inverse:
        sine = -sine
    return jnp.stack([jnp.stack([cosine, -sine]), jnp.stack([sine, cosine])])


def complex_product(left_re, left_im, right_re, right_im):
    return (left_re * right_re - left_im * right_im, left_re * right_im + left_im * right_re)


def compress(echoes, toeplitz, first_pulse, live_pulses, block_cols, window):
    pulse_rows = echoes.shape[1]
    parts_re = []
    parts_im = []
    for start in range(0, RNG, block_cols):
        segment = echoes[:, :, start : start + window]
        stacked = jnp.concatenate([segment[0], segment[1]], axis=1)
        result = lax.dot_general(
            toeplitz, stacked, (((1,), (1,)), ((), ())), preferred_element_type=jnp.float32
        )
        parts_re.append(result[:block_cols])
        parts_im.append(result[block_cols:])
    joined = jnp.stack([jnp.concatenate(parts_re, axis=0), jnp.concatenate(parts_im, axis=0)])
    pulse_ids = first_pulse + jnp.arange(pulse_rows, dtype=jnp.int32)
    keep = (pulse_ids < live_pulses).astype(jnp.float32)
    return (joined * keep[None, None, :]).astype(jnp.bfloat16)


def azimuth(turned, azimuth_rate):
    columns = turned.shape[1]
    length = turned.shape[2]
    outer_len = 64
    inner_len = length // outer_len
    highest = lax.Precision.HIGHEST
    signal = turned.astype(jnp.float32).reshape(2, columns, outer_len, inner_len)
    section_one = jnp.einsum(
        "pcab,pqak->qckb", signal, part_tables(outer_len, False), precision=highest
    )
    outer_ids = jnp.arange(outer_len, dtype=jnp.int32)
    inner_ids = jnp.arange(inner_len, dtype=jnp.int32)
    twist = (
        2.0
        * jnp.pi
        * (outer_ids[:, None] * inner_ids[None, :] % length).astype(jnp.float32)
        / length
    )
    twist_cos = jnp.cos(twist)
    twist_sin = jnp.sin(twist)
    turned_re, turned_im = complex_product(section_one[0], section_one[1], twist_cos, -twist_sin)
    spectrum = jnp.einsum(
        "pckb,pqbm->qckm",
        jnp.stack([turned_re, turned_im]),
        part_tables(inner_len, False),
        precision=highest,
    )
    freq_index = outer_ids[:, None] + outer_len * inner_ids[None, :]
    signed = jnp.where(freq_index < length // 2, freq_index, freq_index - length).astype(
        jnp.float32
    )
    quad = signed * signed / length
    phase = (jnp.pi * azimuth_rate)[:, None, None] * quad[None, :, :]
    filt_re, filt_im = complex_product(spectrum[0], spectrum[1], jnp.cos(phase), -jnp.sin(phase))
    back_one = jnp.einsum(
        "pckm,pqmb->qckb",
        jnp.stack([filt_re, filt_im]),
        part_tables(inner_len, True),
        precision=highest,
    )
    undo_re, undo_im = complex_product(back_one[0], back_one[1], twist_cos, twist_sin)
    restored = jnp.einsum(
        "pckb,pqka->qcab",
        jnp.stack([undo_re, undo_im]),
        part_tables(outer_len, True),
        precision=highest,
    )
    return (restored / length).reshape(2, columns, length)


def parity(index):
    return bin(index).count("1") % 2


def multilook(stacked):
    count, columns, pulse_len = stacked.shape
    inner = 128
    shaped = stacked.reshape(count, columns // LOOK_RNG, LOOK_RNG, pulse_len // inner, inner)
    summed = jnp.sum(shaped, axis=2)
    lanes = jnp.arange(inner, dtype=jnp.int32)
    groups = jnp.arange(inner // LOOK_AZ, dtype=jnp.int32)
    pool = (lanes[:, None] // LOOK_AZ == groups[None, :]).astype(jnp.float32)
    looked = jnp.einsum("nrab,bg->nrag", summed, pool, precision=lax.Precision.HIGHEST)
    scale = 1.0 / (LOOK_RNG * LOOK_AZ)
    return looked.reshape(count, columns // LOOK_RNG, pulse_len // LOOK_AZ) * scale


def cross_looks(own_block, partners):
    own_f = own_block.astype(jnp.float32)
    prods = []
    for partner in partners:
        other_f = partner.astype(jnp.float32)
        prods.append(own_f[0] * other_f[0] + own_f[1] * other_f[1])
        prods.append(own_f[1] * other_f[0] - own_f[0] * other_f[1])
    looked = multilook(jnp.stack(prods))
    return looked.reshape(len(partners), 2, *looked.shape[1:])


def per_device(raw_echo, chirp_phase, pulse_counts, azimuth_rate, partner_bits):
    echoes = raw_echo[0]
    pulses_dev = echoes.shape[1]
    block_cols = min(256, RNG)
    window = block_cols + TAPS - 1
    amplitude = 2.0 / math.sqrt(TAPS)
    table_re = (amplitude * jnp.cos(chirp_phase)).astype(jnp.bfloat16)
    table_im = (amplitude * jnp.sin(chirp_phase)).astype(jnp.bfloat16)
    padding = jnp.zeros((block_cols,), jnp.bfloat16)
    band_re = jnp.tile(jnp.concatenate([table_re, padding]), block_cols)[
        : block_cols * window
    ].reshape(block_cols, window)
    band_im = jnp.tile(jnp.concatenate([table_im, padding]), block_cols)[
        : block_cols * window
    ].reshape(block_cols, window)
    toeplitz = jnp.concatenate(
        [jnp.concatenate([band_re, band_im], axis=1), jnp.concatenate([-band_im, band_re], axis=1)],
        axis=0,
    )
    live_pulses = pulse_counts[0]
    first_pulse = lax.axis_index("pulse") * pulses_dev
    compressed = compress(echoes, toeplitz, first_pulse, live_pulses, block_cols, window)
    turned = lax.all_to_all(compressed, "pulse", split_axis=1, concat_axis=2, tiled=True)
    focused = azimuth(turned, azimuth_rate).astype(jnp.bfloat16)
    chosen = partner_bits[0]
    acq_size = lax.axis_size("acq")
    me = lax.axis_index("acq")
    me_parity = jnp.int32(0)
    for which in range(acq_size.bit_length() - 1):
        me_parity = me_parity ^ me >> which & 1
    low_bits = (0, 1)
    high_bits = (2, 3)
    edge_pairs = []
    for slot in range(2):
        edge_pairs.append(
            [
                (i, i ^ 1 << (high_bits[slot] if parity(i) else low_bits[slot]))
                for i in range(acq_size)
            ]
        )
    arrived = [lax.ppermute(focused, "acq", pairs) for pairs in edge_pairs]
    looked = cross_looks(focused, arrived)
    returned = [
        lax.ppermute(looked[slot], "acq", [(dst, src) for src, dst in edge_pairs[slot]])
        for slot in range(2)
    ]
    candidates = []
    for slot in range(2):
        recv_bit = jnp.where(me_parity == 1, low_bits[slot], high_bits[slot])
        send_bit = jnp.where(me_parity == 1, high_bits[slot], low_bits[slot])
        candidates.append((recv_bit, looked[slot]))
        back = returned[slot]
        candidates.append((send_bit, jnp.stack([back[0], -back[1]])))
    results = []
    for slot in range(2):
        pick = candidates[0][1]
        for bit, value in candidates[1:]:
            pick = jnp.where(chosen[slot] == bit, value, pick)
        results.append(pick)
    interfere_real = jnp.stack([item[0] for item in results])[None]
    interfere_imag = jnp.stack([item[1] for item in results])[None]
    return (interfere_real, interfere_imag)


def solution(mesh):
    in_specs = (P("acq", None, "pulse", None), P(), P("acq"), P("pulse"), P("acq", None))
    out_specs = (P("acq", None, "pulse", None), P("acq", None, "pulse", None))
    return jax.shard_map(
        per_device, mesh=mesh, in_specs=in_specs, out_specs=out_specs, check_vma=False
    )
```

profile of v0, /device:TPU:36, one launch (start us, length us, event | category | flops | bytes accessed | tf_op | source)
XLA Modules:
  0.0 113.7 jit_solution(9805634354367197942)
XLA Ops:
  0.6 0.7 multiply_convert_fusion
  1.4 0.8 tile.21
  2.2 1.2 %reshape.341 = bf16[256,1279]{1,0:T(8,128)(2,1)S(1)} reshape(bf16[327424]{0:T(1024)(128)(2,1)S(1)} %bitcast.138) | data formatting | bytes 1309696 | tf_op jit(solution)/shard_map/reshape | solution.py:137
  3.4 1.0 neg.61
  4.4 3.6 %copy.30 = bf16[1,2,256,1535]{3,2,1,0:T(8,128)(2,1)S(1)} copy(bf16[1,2,256,1535]{2,1,3,0:T(2,128)(2,1)} %param.5) | data formatting | bytes 3143680 | tf_op args[0]
  8.0 1.2 %slice_bitcast_fusion.3 = (bf16[256,1279]{1,0:T(8,128)(2,1)}, bf16[256,1279]{1,0:T(8,128)(2,1)S(1)}, bf16[256,1279]{1,0:T(8,128)(2,1)S(1)}, bf16[256,1279]{1,0:T(8,128)(2,1)}) fusion(bf16[2,256,1535]{2,1,0:T(8,128)(2,1)S(1)} %bitcast.137), kind=kLoop, calls=%fused_computation.38 | loop fusion | bytes 5238784 | tf_op jit(solution)/shard_map/squeeze | solution.py:33
  9.3 0.8 tile.9
  10.1 2.1 %reshape.340 = bf16[256,1279]{1,0:T(8,128)(2,1)} reshape(bf16[327424]{0:T(1024)(128)(2,1)S(1)} %bitcast.139) | data formatting | bytes 1309696 | tf_op jit(solution)/shard_map/reshape | solution.py:134
  12.1 3.0 %fusion.2 = f32[512,256]{1,0:T(8,128)S(1)} fusion(bf16[256,1279]{1,0:T(8,128)(2,1)} %get-tuple-element.9, bf16[256,1279]{1,0:T(8,128)(2,1)} %get-tuple-element.6, bf16[256,1279]{1,0:T(8,128)(2,1)} %reshape.340, bf16[256,1279]{1,0:T(8,128)(2,1)} %neg.61, bf16[256,1279]{1,0:T(8,128)(2,1)S(1)} %reshape.341), kind=kOutput, calls=%fused_computation.9 | convolution fusion | flops 683661312 | bytes 3798528 | tf_op jit(solution)/shard_map/dot_general | solution.py:34
  15.2 1.0 fusion.6
  17.1 1.4 %copy.31 = bf16[2,512,256]{2,0,1:T(2,128)(2,1)} copy(bf16[2,512,256]{2,1,0:T(8,128)(2,1)S(1)} %fusion.12) | data formatting | bytes 1048576 | tf_op jit(solution)/shard_map/convert_element_type | solution.py:42
  18.5 18.0 %all-to-all-start = ((bf16[2,512,256]{2,0,1:T(2,128)(2,1)}), bf16[2,512,256]{2,0,1:T(2,128)(2,1)S(1)}, u32[]{:S(2)}, u32[]{:S(2)}) async-start(bf16[2,512,256]{2,0,1:T(2,128)(2,1)} %copy.31), calls=%async_computation | async-start | bytes 1048576 | tf_op jit(solution)/shard_map/all_to_all | solution.py:145
  37.7 32.5 %all-to-all-done = bf16[2,512,256]{2,0,1:T(2,128)(2,1)S(1)} async-done(((bf16[2,512,256]{2,0,1:T(2,128)(2,1)}), bf16[2,512,256]{2,0,1:T(2,128)(2,1)S(1)}, u32[]{:S(2)}, u32[]{:S(2)}) %all-to-all-start) | async-done | bytes 524320 | tf_op jit(solution)/shard_map/all_to_all | solution.py:145
  71.5 1.0 convolution_bitcast_fusion.2
  72.5 2.1 %fusion.23 = (f32[1,16,64,128]{3,2,1,0:T(8,128)S(1)}, f32[1,16,64,128]{3,2,1,0:T(8,128)S(1)}) fusion(f32[2,16,64,128]{3,2,1,0:T(8,128)S(1)} %convolution_bitcast_fusion.2, f32[64,128]{1,0:T(8,128)S(1)} %fusion.56, f32[16]{0:T(128)S(1)} %broadcast_multiply_fusion), kind=kLoop, calls=%fused_computation.39 | loop fusion | flops 1048576 | bytes 2129984 | tf_op jit(solution)/shard_map/sub | solution.py:24
  74.6 1.0 convolution_bitcast_fusion.1
  75.8 1.1 fusion.11
  77.1 2.4 %collective-permute-start = (bf16[2,16,8192]{2,1,0:T(8,128)(2,1)S(1)}, bf16[2,16,8192]{2,1,0:T(8,128)(2,1)S(1)}, u32[]{:S(2)}, u32[]{:S(2)}) collective-permute-start(bf16[2,16,8192]{2,1,0:T(8,128)(2,1)S(1)} %convert_element_type.148), channel_id=1, source_target_pairs={{0,32},{32,160},{64,192},{96,64},{128,0},{160,128},{192,224},{224,... | collective-permute-start | bytes 1572872 | tf_op jit(solution)/shard_map/ppermute | solution.py:163
  79.6 2.1 %collective-permute-start.1 = (bf16[2,16,8192]{2,1,0:T(8,128)(2,1)S(1)}, bf16[2,16,8192]{2,1,0:T(8,128)(2,1)S(1)}, u32[]{:S(2)}, u32[]{:S(2)}) collective-permute-start(bf16[2,16,8192]{2,1,0:T(8,128)(2,1)S(1)} %convert_element_type.148), channel_id=1, source_target_pairs={{0,64},{32,288},{64,320},{96,32},{128,384},{160,224},{192,128},{22... | collective-permute-start | bytes 1572872 | tf_op jit(solution)/shard_map/ppermute | solution.py:163
  81.7 8.8 %collective-permute-done = bf16[2,16,8192]{2,1,0:T(8,128)(2,1)S(1)} collective-permute-done((bf16[2,16,8192]{2,1,0:T(8,128)(2,1)S(1)}, bf16[2,16,8192]{2,1,0:T(8,128)(2,1)S(1)}, u32[]{:S(2)}, u32[]{:S(2)}) %collective-permute-start) | collective-permute-done | bytes 524320 | tf_op jit(solution)/shard_map/ppermute | solution.py:163
  92.2 0.7 convolution_multiply_fusion
  93.3 7.2 %collective-permute-start.2 = (f32[2,4,512]{2,1,0:T(4,128)S(1)}, f32[2,4,512]{2,1,0:T(4,128)S(1)}, u32[]{:S(2)}, u32[]{:S(2)}) collective-permute-start(f32[2,4,512]{2,1,0:T(4,128)S(1)} %slice.158), channel_id=1, source_target_pairs={{64,0},{288,32},{320,64},{32,96},{384,128},{224,160},{128,192},{48... | collective-permute-start | bytes 49160 | tf_op jit(solution)/shard_map/ppermute | solution.py:166
  105.3 1.9 %collective-permute-start.3 = (f32[2,4,512]{2,1,0:T(4,128)S(1)}, f32[2,4,512]{2,1,0:T(4,128)S(1)}, u32[]{:S(2)}, u32[]{:S(2)}) collective-permute-start(f32[2,4,512]{2,1,0:T(4,128)S(1)} %slice.162), channel_id=1, source_target_pairs={{32,0},{160,32},{192,64},{64,96},{0,128},{128,160},{224,192},{96,2... | collective-permute-start | bytes 49160 | tf_op jit(solution)/shard_map/ppermute | solution.py:166
  107.2 5.2 %collective-permute-done.3 = f32[2,4,512]{2,1,0:T(4,128)S(1)} collective-permute-done((f32[2,4,512]{2,1,0:T(4,128)S(1)}, f32[2,4,512]{2,1,0:T(4,128)S(1)}, u32[]{:S(2)}, u32[]{:S(2)}) %collective-permute-start.3) | collective-permute-done | bytes 16416 | tf_op jit(solution)/shard_map/ppermute | solution.py:166
  (59 shorter events, 7.3 us)
Async XLA Ops:
  12.1 3.0 %copy-start = (bf16[256,1279]{1,0:T(8,128)(2,1)S(1)}, bf16[256,1279]{1,0:T(8,128)(2,1)}, u32[]{:S(2)}) copy-start(bf16[256,1279]{1,0:T(8,128)(2,1)} %neg.61) | copy-start | bytes 1964548
  12.1 3.1 %copy-start.1 = (bf16[256,1279]{1,0:T(8,128)(2,1)S(1)}, bf16[256,1279]{1,0:T(8,128)(2,1)}, u32[]{:S(2)}) copy-start(bf16[256,1279]{1,0:T(8,128)(2,1)} %reshape.340) | copy-start | bytes 1964548
  17.1 20.6 %copy-start.3 = (f32[16]{0:T(128)S(1)}, f32[16]{0:T(128)}, u32[]{:S(2)}) copy-start(f32[16]{0:T(128)} %param.8) | copy-start | bytes 196
  18.5 51.7 %all-to-all-start = ((bf16[2,512,256]{2,0,1:T(2,128)(2,1)}), bf16[2,512,256]{2,0,1:T(2,128)(2,1)S(1)}, u32[]{:S(2)}, u32[]{:S(2)}) async-start(bf16[2,512,256]{2,0,1:T(2,128)(2,1)} %copy.31), calls=%async_computation | async-start | bytes 1048576 | tf_op jit(solution)/shard_map/all_to_all | solution.py:145
  77.1 13.5 %collective-permute-start = (bf16[2,16,8192]{2,1,0:T(8,128)(2,1)S(1)}, bf16[2,16,8192]{2,1,0:T(8,128)(2,1)S(1)}, u32[]{:S(2)}, u32[]{:S(2)}) collective-permute-start(bf16[2,16,8192]{2,1,0:T(8,128)(2,1)S(1)} %convert_element_type.148), channel_id=1, source_target_pairs={{0,32},{32,160},{64,192},{96,64},{128,0},{160,128},{192,224},{224,... | collective-permute-start | bytes 1572872 | tf_op jit(solution)/shard_map/ppermute | solution.py:163
  79.6 11.7 %collective-permute-start.1 = (bf16[2,16,8192]{2,1,0:T(8,128)(2,1)S(1)}, bf16[2,16,8192]{2,1,0:T(8,128)(2,1)S(1)}, u32[]{:S(2)}, u32[]{:S(2)}) collective-permute-start(bf16[2,16,8192]{2,1,0:T(8,128)(2,1)S(1)} %convert_element_type.148), channel_id=1, source_target_pairs={{0,64},{32,288},{64,320},{96,32},{128,384},{160,224},{192,128},{22... | collective-permute-start | bytes 1572872 | tf_op jit(solution)/shard_map/ppermute | solution.py:163
  92.0 8.5 %copy-start.2 = (s32[1,2]{1,0:T(1,128)S(1)}, s32[1,2]{1,0:T(1,128)}, u32[]{:S(2)}) copy-start(s32[1,2]{1,0:T(1,128)} %param.9) | copy-start | bytes 28
  93.3 13.9 %collective-permute-start.2 = (f32[2,4,512]{2,1,0:T(4,128)S(1)}, f32[2,4,512]{2,1,0:T(4,128)S(1)}, u32[]{:S(2)}, u32[]{:S(2)}) collective-permute-start(f32[2,4,512]{2,1,0:T(4,128)S(1)} %slice.158), channel_id=1, source_target_pairs={{64,0},{288,32},{320,64},{32,96},{384,128},{224,160},{128,192},{48... | collective-permute-start | bytes 49160 | tf_op jit(solution)/shard_map/ppermute | solution.py:166
  105.3 7.1 %collective-permute-start.3 = (f32[2,4,512]{2,1,0:T(4,128)S(1)}, f32[2,4,512]{2,1,0:T(4,128)S(1)}, u32[]{:S(2)}, u32[]{:S(2)}) collective-permute-start(f32[2,4,512]{2,1,0:T(4,128)S(1)} %slice.162), channel_id=1, source_target_pairs={{32,0},{160,32},{192,64},{64,96},{0,128},{128,160},{224,192},{96,2... | collective-permute-start | bytes 49160 | tf_op jit(solution)/shard_map/ppermute | solution.py:166
where the time goes:
time: 114 us
  waiting for transfers between devices  47.1 us (41%)
  starting transfers between devices  31.6 us (28%)
  local copies, waits for them, and re-layouts  13.5 us (12%)
  matrix products  8.41 us (7%)
  other arithmetic  7.39 us (6%)
  between operations  5.63 us (5%)
    all_to_all x1, waiting for transfers between devices, per_device(): lax.all_to_all(compressed, 'pulse', split_axis=1, concat_axis=2, tiled=True)  32.5 us
    all_to_all x1, starting transfers between devices, per_device(): lax.all_to_all(compressed, 'pulse', split_axis=1, concat_axis=2, tiled=True)  18 us
    ppermute x2, waiting for transfers between devices, per_device(): arrived = [lax.ppermute(focused, 'acq', pairs) for pairs in edge_pairs]  9.46 us
    ppermute x2, starting transfers between devices, per_device(): lax.ppermute(looked[slot], 'acq', [(dst, src) for src, dst in edge_pairs[...  9.13 us
    ppermute x2, waiting for transfers between devices, per_device(): lax.ppermute(looked[slot], 'acq', [(dst, src) for src, dst in edge_pairs[...  5.19 us
    ppermute x2, starting transfers between devices, per_device(): arrived = [lax.ppermute(focused, 'acq', pairs) for pairs in edge_pairs]  4.51 us
    unnamed x13, local copies, waits for them, and re-layouts  4.04 us
    dot_general x2, matrix products, compress(): lax.dot_general(toeplitz, stacked, (((1,), (1,)), ((), ())), preferred_el...  3.99 us
  transfers between devices with their start and end apart: 5, of which 4 were waited for; matrix products, arithmetic and copies ran while one was open for 2% of the time, Pallas kernels for 0%

commit v1 on v0

--- a/solution.py
+++ b/solution.py
@@ -142,7 +142,12 @@
     live_pulses = pulse_counts[0]
     first_pulse = lax.axis_index("pulse") * pulses_dev
     compressed = compress(echoes, toeplitz, first_pulse, live_pulses, block_cols, window)
-    turned = lax.all_to_all(compressed, "pulse", split_axis=1, concat_axis=2, tiled=True)
+    turned = jnp.concatenate(
+        lax.all_to_all(
+            jnp.stack(jnp.split(compressed, lax.axis_size("pulse"), axis=1)), "pulse", 0, 0
+        ),
+        axis=2,
+    )
     focused = azimuth(turned, azimuth_rate).astype(jnp.bfloat16)
     chosen = partner_bits[0]
     acq_size = lax.axis_size("acq")

time: 114 us -> 132 us (1.16)
  local copies, waits for them, and re-layouts: 13.5 us -> 31.3 us
    unnamed x13 -> x44, local copies, waits for them, and re-layouts: 4.04 us -> 22.6 us
    convert_element_type x1 -> x0, local copies, waits for them, and re-layouts: 1.35 us -> none  [compress(): return (joined * keep[None, None, :]).astype(jnp.bfloat16)]
where the time goes in v1:
time: 132 us; the launch traced here: 131 us
  waiting for transfers between devices  47.1 us (36%)
  starting transfers between devices  31.6 us (24%)
  local copies, waits for them, and re-layouts  31.3 us (24%)
  matrix products  8.43 us (6%)
  other arithmetic  7.39 us (6%)
  between operations  5.64 us (4%)
    all_to_all x1, waiting for transfers between devices, per_device(): lax.all_to_all(jnp.stack(jnp.split(compressed, lax.axis_size('pulse'), ax...  32.5 us
    unnamed x44, local copies, waits for them, and re-layouts  22.6 us
    all_to_all x1, starting transfers between devices, per_device(): lax.all_to_all(jnp.stack(jnp.split(compressed, lax.axis_size('pulse'), ax...  18 us
    ppermute x2, waiting for transfers between devices, per_device(): arrived = [lax.ppermute(focused, 'acq', pairs) for pairs in edge_pairs]  9.45 us
    ppermute x2, starting transfers between devices, per_device(): lax.ppermute(looked[slot], 'acq', [(dst, src) for src, dst in edge_pairs[...  9.11 us
    ppermute x2, waiting for transfers between devices, per_device(): lax.ppermute(looked[slot], 'acq', [(dst, src) for src, dst in edge_pairs[...  5.19 us
    ppermute x2, starting transfers between devices, per_device(): arrived = [lax.ppermute(focused, 'acq', pairs) for pairs in edge_pairs]  4.5 us
    dot_general x2, matrix products, compress(): lax.dot_general(toeplitz, stacked, (((1,), (1,)), ((), ())), preferred_el...  3.99 us
  transfers between devices with their start and end apart: 5, of which 4 were waited for; matrix products, arithmetic and copies ran while one was open for 2% of the time, Pallas kernels for 0%

profile of v1, /device:TPU:36, one launch (start us, length us, event | category | flops | bytes accessed | tf_op | source)
XLA Modules:
  0.0 131.5 jit_solution(7584870578271528940)
XLA Ops:
  0.6 0.7 multiply_convert_fusion
  1.4 0.8 tile.21
  2.2 1.2 reshape.345
  3.4 1.0 neg.61
  4.4 3.6 %copy.18 = bf16[1,2,256,1535]{3,2,1,0:T(8,128)(2,1)S(1)} copy(bf16[1,2,256,1535]{2,1,3,0:T(2,128)(2,1)} %param.5) | data formatting | bytes 3143680 | tf_op args[0]
  8.0 1.2 slice_bitcast_fusion.3
  9.3 0.8 tile.9
  10.1 2.1 %reshape.344 = bf16[256,1279]{1,0:T(8,128)(2,1)} reshape(bf16[327424]{0:T(1024)(128)(2,1)S(1)} %bitcast.264) | data formatting | bytes 1309696 | tf_op jit(solution)/shard_map/reshape | solution.py:134
  12.1 3.0 %fusion.2 = f32[512,256]{1,0:T(8,128)S(1)} fusion(bf16[256,1279]{1,0:T(8,128)(2,1)} %get-tuple-element.9, bf16[256,1279]{1,0:T(8,128)(2,1)} %get-tuple-element.6, bf16[256,1279]{1,0:T(8,128)(2,1)} %reshape.344, bf16[256,1279]{1,0:T(8,128)(2,1)} %neg.61, bf16[256,1279]{1,0:T(8,128)(2,1)S(1)} %reshape.345), kind=kOutput, calls=%fused_computation.9 | convolution fusion | flops 683661312 | bytes 3798528 | tf_op jit(solution)/shard_map/dot_general | solution.py:34
  15.2 1.0 fusion.6
  36.3 18.0 %all-to-all-start = ((bf16[32,2,16,256]{3,2,1,0:T(8,128)(2,1)}), bf16[32,2,16,256]{3,2,1,0:T(8,128)(2,1)S(1)}, u32[]{:S(2)}, u32[]{:S(2)}) async-start(bf16[32,2,16,256]{3,2,1,0:T(8,128)(2,1)} %constant_dynamic-update-slice_fusion), calls=%async_computation | async-start | bytes 1048576 | tf_op jit(solution)/shard_map/all_to_all | solution.py:146
  55.6 32.5 %all-to-all-done = bf16[32,2,16,256]{3,2,1,0:T(8,128)(2,1)S(1)} async-done(((bf16[32,2,16,256]{3,2,1,0:T(8,128)(2,1)}), bf16[32,2,16,256]{3,2,1,0:T(8,128)(2,1)S(1)}, u32[]{:S(2)}, u32[]{:S(2)}) %all-to-all-start) | async-done | bytes 524320 | tf_op jit(solution)/shard_map/all_to_all | solution.py:146
  89.3 1.0 convolution_bitcast_fusion.2
  90.3 2.1 %fusion.23 = (f32[1,16,64,128]{3,2,1,0:T(8,128)S(1)}, f32[1,16,64,128]{3,2,1,0:T(8,128)S(1)}) fusion(f32[2,16,64,128]{3,2,1,0:T(8,128)S(1)} %convolution_bitcast_fusion.2, f32[64,128]{1,0:T(8,128)S(1)} %fusion.56, f32[16]{0:T(128)S(1)} %broadcast_multiply_fusion), kind=kLoop, calls=%fused_computation.39 | loop fusion | flops 1048576 | bytes 2129984 | tf_op jit(solution)/shard_map/sub | solution.py:24
  92.5 1.0 convolution_bitcast_fusion.1
  93.7 1.1 fusion.11
  95.0 2.4 %collective-permute-start = (bf16[2,16,8192]{2,1,0:T(8,128)(2,1)S(1)}, bf16[2,16,8192]{2,1,0:T(8,128)(2,1)S(1)}, u32[]{:S(2)}, u32[]{:S(2)}) collective-permute-start(bf16[2,16,8192]{2,1,0:T(8,128)(2,1)S(1)} %convert_element_type.148), channel_id=1, source_target_pairs={{0,32},{32,160},{64,192},{96,64},{128,0},{160,128},{192,224},{224,... | collective-permute-start | bytes 1572872 | tf_op jit(solution)/shard_map/ppermute | solution.py:168
  97.4 2.1 %collective-permute-start.1 = (bf16[2,16,8192]{2,1,0:T(8,128)(2,1)S(1)}, bf16[2,16,8192]{2,1,0:T(8,128)(2,1)S(1)}, u32[]{:S(2)}, u32[]{:S(2)}) collective-permute-start(bf16[2,16,8192]{2,1,0:T(8,128)(2,1)S(1)} %convert_element_type.148), channel_id=1, source_target_pairs={{0,64},{32,288},{64,320},{96,32},{128,384},{160,224},{192,128},{22... | collective-permute-start | bytes 1572872 | tf_op jit(solution)/shard_map/ppermute | solution.py:168
  99.6 8.8 %collective-permute-done = bf16[2,16,8192]{2,1,0:T(8,128)(2,1)S(1)} collective-permute-done((bf16[2,16,8192]{2,1,0:T(8,128)(2,1)S(1)}, bf16[2,16,8192]{2,1,0:T(8,128)(2,1)S(1)}, u32[]{:S(2)}, u32[]{:S(2)}) %collective-permute-start) | collective-permute-done | bytes 524320 | tf_op jit(solution)/shard_map/ppermute | solution.py:168
  108.4 0.7 collective-permute-done.1
  110.1 0.7 convolution_multiply_fusion
  111.1 7.2 %collective-permute-start.2 = (f32[2,4,512]{2,1,0:T(4,128)S(1)}, f32[2,4,512]{2,1,0:T(4,128)S(1)}, u32[]{:S(2)}, u32[]{:S(2)}) collective-permute-start(f32[2,4,512]{2,1,0:T(4,128)S(1)} %slice.158), channel_id=1, source_target_pairs={{64,0},{288,32},{320,64},{32,96},{384,128},{224,160},{128,192},{48... | collective-permute-start | bytes 49160 | tf_op jit(solution)/shard_map/ppermute | solution.py:171
  123.1 1.9 %collective-permute-start.3 = (f32[2,4,512]{2,1,0:T(4,128)S(1)}, f32[2,4,512]{2,1,0:T(4,128)S(1)}, u32[]{:S(2)}, u32[]{:S(2)}) collective-permute-start(f32[2,4,512]{2,1,0:T(4,128)S(1)} %slice.162), channel_id=1, source_target_pairs={{32,0},{160,32},{192,64},{64,96},{0,128},{128,160},{224,192},{96,2... | collective-permute-start | bytes 49160 | tf_op jit(solution)/shard_map/ppermute | solution.py:171
  125.0 5.2 %collective-permute-done.3 = f32[2,4,512]{2,1,0:T(4,128)S(1)} collective-permute-done((f32[2,4,512]{2,1,0:T(4,128)S(1)}, f32[2,4,512]{2,1,0:T(4,128)S(1)}, u32[]{:S(2)}, u32[]{:S(2)}) %collective-permute-start.3) | collective-permute-done | bytes 16416 | tf_op jit(solution)/shard_map/ppermute | solution.py:171
  (90 shorter events, 25.9 us)
Async XLA Ops:
  12.1 3.0 %copy-start = (bf16[256,1279]{1,0:T(8,128)(2,1)S(1)}, bf16[256,1279]{1,0:T(8,128)(2,1)}, u32[]{:S(2)}) copy-start(bf16[256,1279]{1,0:T(8,128)(2,1)} %neg.61) | copy-start | bytes 1964548
  12.1 3.1 %copy-start.1 = (bf16[256,1279]{1,0:T(8,128)(2,1)S(1)}, bf16[256,1279]{1,0:T(8,128)(2,1)}, u32[]{:S(2)}) copy-start(bf16[256,1279]{1,0:T(8,128)(2,1)} %reshape.344) | copy-start | bytes 1964548
  24.9 30.6 %copy-start.3 = (f32[16]{0:T(128)S(1)}, f32[16]{0:T(128)}, u32[]{:S(2)}) copy-start(f32[16]{0:T(128)} %param.8) | copy-start | bytes 196
  36.3 51.7 %all-to-all-start = ((bf16[32,2,16,256]{3,2,1,0:T(8,128)(2,1)}), bf16[32,2,16,256]{3,2,1,0:T(8,128)(2,1)S(1)}, u32[]{:S(2)}, u32[]{:S(2)}) async-start(bf16[32,2,16,256]{3,2,1,0:T(8,128)(2,1)} %constant_dynamic-update-slice_fusion), calls=%async_computation | async-start | bytes 1048576 | tf_op jit(solution)/shard_map/all_to_all | solution.py:146
  95.0 13.4 %collective-permute-start = (bf16[2,16,8192]{2,1,0:T(8,128)(2,1)S(1)}, bf16[2,16,8192]{2,1,0:T(8,128)(2,1)S(1)}, u32[]{:S(2)}, u32[]{:S(2)}) collective-permute-start(bf16[2,16,8192]{2,1,0:T(8,128)(2,1)S(1)} %convert_element_type.148), channel_id=1, source_target_pairs={{0,32},{32,160},{64,192},{96,64},{128,0},{160,128},{192,224},{224,... | collective-permute-start | bytes 1572872 | tf_op jit(solution)/shard_map/ppermute | solution.py:168
  97.4 11.7 %collective-permute-start.1 = (bf16[2,16,8192]{2,1,0:T(8,128)(2,1)S(1)}, bf16[2,16,8192]{2,1,0:T(8,128)(2,1)S(1)}, u32[]{:S(2)}, u32[]{:S(2)}) collective-permute-start(bf16[2,16,8192]{2,1,0:T(8,128)(2,1)S(1)} %convert_element_type.148), channel_id=1, source_target_pairs={{0,64},{32,288},{64,320},{96,32},{128,384},{160,224},{192,128},{22... | collective-permute-start | bytes 1572872 | tf_op jit(solution)/shard_map/ppermute | solution.py:168
  109.9 8.4 %copy-start.2 = (s32[1,2]{1,0:T(1,128)S(1)}, s32[1,2]{1,0:T(1,128)}, u32[]{:S(2)}) copy-start(s32[1,2]{1,0:T(1,128)} %param.9) | copy-start | bytes 28
  111.1 13.9 %collective-permute-start.2 = (f32[2,4,512]{2,1,0:T(4,128)S(1)}, f32[2,4,512]{2,1,0:T(4,128)S(1)}, u32[]{:S(2)}, u32[]{:S(2)}) collective-permute-start(f32[2,4,512]{2,1,0:T(4,128)S(1)} %slice.158), channel_id=1, source_target_pairs={{64,0},{288,32},{320,64},{32,96},{384,128},{224,160},{128,192},{48... | collective-permute-start | bytes 49160 | tf_op jit(solution)/shard_map/ppermute | solution.py:171
  123.1 7.1 %collective-permute-start.3 = (f32[2,4,512]{2,1,0:T(4,128)S(1)}, f32[2,4,512]{2,1,0:T(4,128)S(1)}, u32[]{:S(2)}, u32[]{:S(2)}) collective-permute-start(f32[2,4,512]{2,1,0:T(4,128)S(1)} %slice.162), channel_id=1, source_target_pairs={{32,0},{160,32},{192,64},{64,96},{0,128},{128,160},{224,192},{96,2... | collective-permute-start | bytes 49160 | tf_op jit(solution)/shard_map/ppermute | solution.py:171
